TPU v7x, 32 devices: a whole 2x2x4 slice. The times are simulated.
32 devices in a mesh: dp: 2 (over y), expert: 16 (over z, x, core).
Axes of the slice: x: 2, y: 2, z: 4, core: 2. Of those that a mesh axis runs over, the one named last changes fastest.
Arguments:
- tokens: bfloat16 [2048, 1024], P(('dp', 'expert')), may hold values from -6 to 6
- cotangent: bfloat16 [2048, 1024], P(('dp', 'expert')), may hold values from -6 to 6
- expert_ids: int32 [2048, 6], P(('dp', 'expert')), may hold values from 0 to 15, all different within a row; in each aligned block of 64 rows (0 to 63, 64 to 127, ...) at most 32 rows name the same one
- gate_probs: float32 [2048, 6], P(('dp', 'expert')), may hold values from 0.1 to 1
- w_gate_up: bfloat16 [16, 1024, 1408], P('expert', 'dp'), may hold values from -0.1875 to 0.1875
- w_down: bfloat16 [16, 704, 1024], P('expert'), may hold values from -0.21875 to 0.21875
Outputs:
- layer_out: bfloat16 [2048, 1024], P(('dp', 'expert'))
- input_grad: bfloat16 [2048, 1024], P(('dp', 'expert'))
- prob_grad: float32 [2048, 6], P(('dp', 'expert'))
- gate_up_grad: bfloat16 [16, 1024, 1408], P('expert', 'dp')
Inputs may be any that keep to these rules, and one draw needn't show every extreme that they name: `expert_ids`: each row names 6 different experts. Within each aligned block of 64 rows no expert is named by more than 32 rows, and in some block an expert is named by exactly 32 rows.
All inputs are finite; a program needn't handle non-finite values.
Results may differ from a plain program's by a relative error of at most 0.013.
Values may be sent and summed in bfloat16 or wider, within the bound.
No kernel may reach another device: no remote copies, remote signals or barrier semaphores. Data moves between devices by JAX's collectives and lax.ppermute only.
A program may use at most 64 MiB of HBM per device.

v0:
```python
import jax
import jax.numpy as jnp
from jax import lax
from jax.sharding import PartitionSpec as P


def local(tokens, cotangent, expert_ids, gate_probs, w_gate_up, w_down):
    experts = lax.axis_size("expert")
    token_count = tokens.shape[0]
    model_width = tokens.shape[1]
    top_count = expert_ids.shape[1]
    hidden_units = w_down.shape[1]
    capacity = 4 * token_count * top_count // (3 * experts)
    flat_routes = expert_ids.reshape(token_count * top_count)
    onehot = (flat_routes[:, None] == jnp.arange(experts, dtype=jnp.int32)[None, :]).astype(
        jnp.int32
    )
    before = jnp.cumsum(onehot, axis=0) - onehot
    slot_rank = jnp.sum(before * onehot, axis=1)
    target_rows = flat_routes * capacity + slot_rank
    token_copies = jnp.broadcast_to(tokens[:, None, :], (token_count, top_count, model_width))
    token_copies = token_copies.reshape(token_count * top_count, model_width)
    cot_copies = (gate_probs[:, :, None] * cotangent[:, None, :].astype(jnp.float32)).astype(
        jnp.bfloat16
    )
    cot_copies = cot_copies.reshape(token_count * top_count, model_width)
    token_send = (
        jnp.zeros((experts * capacity, model_width), jnp.bfloat16).at[target_rows].set(token_copies)
    )
    cot_send = (
        jnp.zeros((experts * capacity, model_width), jnp.bfloat16).at[target_rows].set(cot_copies)
    )
    token_send = token_send.reshape(experts, capacity, model_width)
    cot_send = cot_send.reshape(experts, capacity, model_width)
    token_recv, cot_early = (
        lax.all_to_all(token_send, "expert", split_axis=0, concat_axis=0, tiled=True),
        lax.all_to_all(cot_send, "expert", split_axis=0, concat_axis=0, tiled=True),
    )
    input_rows = token_recv.reshape(experts * capacity, model_width)
    weight_down = w_down[0]
    weight_fwd = lax.all_gather(w_gate_up, "dp", axis=1, tiled=True)[0]
    gate_up = jnp.dot(input_rows, weight_fwd, preferred_element_type=jnp.float32)
    gate = gate_up[:, :hidden_units]
    upper = gate_up[:, hidden_units:]
    sigma = jax.nn.sigmoid(gate)
    active = gate * sigma
    hidden = (active * upper).astype(jnp.bfloat16)
    output_rows = jnp.dot(hidden, weight_down, preferred_element_type=jnp.float32).astype(
        jnp.bfloat16
    )
    cot_rows = cot_early.reshape(experts * capacity, model_width)
    hidden_grad = lax.dot_general(
        cot_rows, weight_down, (((1,), (1,)), ((), ())), preferred_element_type=jnp.float32
    )
    gate_cot = hidden_grad * upper * sigma * (1.0 + gate * (1.0 - sigma))
    upper_cot = hidden_grad * active
    pair_cot = jnp.concatenate([gate_cot, upper_cot], axis=1).astype(jnp.bfloat16)
    input_cot = lax.dot_general(
        pair_cot, weight_fwd, (((1,), (1,)), ((), ())), preferred_element_type=jnp.float32
    ).astype(jnp.bfloat16)
    weight_cot = lax.dot_general(
        input_rows, pair_cot, (((0,), (0,)), ((), ())), preferred_element_type=jnp.float32
    )
    output_back, input_back = (
        lax.all_to_all(
            output_rows.reshape(experts, capacity, model_width),
            "expert",
            split_axis=0,
            concat_axis=0,
            tiled=True,
        ),
        lax.all_to_all(
            input_cot.reshape(experts, capacity, model_width),
            "expert",
            split_axis=0,
            concat_axis=0,
            tiled=True,
        ),
    )
    slot_out = output_back.reshape(experts * capacity, model_width)[target_rows].reshape(
        token_count, top_count, model_width
    )
    slot_in = input_back.reshape(experts * capacity, model_width)[target_rows].reshape(
        token_count, top_count, model_width
    )
    layer_out = jnp.sum(gate_probs[:, :, None] * slot_out.astype(jnp.float32), axis=1).astype(
        jnp.bfloat16
    )
    input_grad = jnp.sum(slot_in.astype(jnp.float32), axis=1).astype(jnp.bfloat16)
    prob_grad = jnp.einsum("td,tkd->tk", cotangent, slot_out, preferred_element_type=jnp.float32)
    grad_rows = lax.psum_scatter(
        weight_cot.astype(jnp.bfloat16), "dp", scatter_dimension=0, tiled=True
    )
    return (layer_out, input_grad, prob_grad, grad_rows[None])


def solution(mesh):
    placed = (
        P(("dp", "expert"), None),
        P(("dp", "expert"), None),
        P(("dp", "expert"), None),
        P(("dp", "expert"), None),
        P("expert", "dp", None),
        P("expert", None, None),
    )
    return jax.shard_map(
        local,
        mesh=mesh,
        in_specs=placed,
        out_specs=(
            P(("dp", "expert"), None),
            P(("dp", "expert"), None),
            P(("dp", "expert"), None),
            P("expert", "dp", None),
        ),
        check_vma=False,
    )
```

profile of v0, /device:TPU:15, one launch (start us, length us, event | category | flops | bytes accessed | tf_op | source)
XLA Modules:
  0.0 166.2 jit_solution(6136234102006525579)
XLA Ops:
  7.2 0.0 copy-start
  7.2 0.8 broadcast_multiply_fusion
  8.0 0.8 copy.15
  8.8 0.1 eq.29
  8.9 0.1 eq.25
  9.0 0.1 copy.14
  9.1 0.1 mul.69
  9.3 0.9 reduce-window.6
  10.2 0.2 slice_reduce_fusion
  10.4 1.1 broadcast_in_dim.4
  11.5 0.3 reshape.126
  11.8 0.1 fusion.21
  11.9 3.1 %scatter_custom_fusion = bf16[512,1024]{1,0:T(8,128)(2,1)} fusion(s32[384]{0:T(512)S(1)} %fusion.23, bf16[384,1024]{1,0:T(8,128)(2,1)S(1)} %reshape.126, bf16[]{:T(256)} %constant.6.clone.1), kind=kCustom, calls=%fused_computation.25 | custom fusion | bytes 1048578 | tf_op jit(solution)/shard_map/scatter | solution.py:28
  15.0 0.0 copy-start.3
  15.0 6.7 %all-to-all-start = ((bf16[16,32,1024]{2,1,0:T(8,128)(2,1)}), bf16[16,32,1024]{2,1,0:T(8,128)(2,1)}, u32[]{:S(2)}, u32[]{:S(2)}) async-start(bf16[16,32,1024]{2,1,0:T(8,128)(2,1)} %bitcast.1), calls=%async_computation | async-start | bytes 2097152 | tf_op jit(solution)/shard_map/all_to_all | solution.py:36
  21.7 0.0 all-gather.2.cloned.1.call-start
  21.7 0.7 all-gather.2.cloned.1.call-update
  22.4 0.0 copy-done.3
  22.4 0.1 copy.13
  22.5 0.0 copy-start.1
  22.5 0.6 copy-done.1
  23.1 0.1 mul.74
  23.2 1.2 mul.76
  24.4 1.4 mul.77
  25.8 4.0 %scatter_custom_fusion.1 = bf16[512,1024]{1,0:T(8,128)(2,1)} fusion(s32[384]{0:T(512)S(1)} %fusion.23, f32[384,1024]{1,0:T(8,128)} %mul.77, f32[384]{0:T(512)S(1)} %mul.74, bf16[]{:T(256)} %constant.6.clone.1), kind=kCustom, calls=%fused_computation.22 | custom fusion | flops 786432 | bytes 2623490 | tf_op jit(solution)/shard_map/scatter | solution.py:31
  29.8 17.2 %all-to-all-done = bf16[16,32,1024]{2,1,0:T(8,128)(2,1)} async-done(((bf16[16,32,1024]{2,1,0:T(8,128)(2,1)}), bf16[16,32,1024]{2,1,0:T(8,128)(2,1)}, u32[]{:S(2)}, u32[]{:S(2)}) %all-to-all-start) | async-done | bytes 1048608 | tf_op jit(solution)/shard_map/all_to_all | solution.py:36
  46.9 4.6 %all-to-all-start.2 = ((bf16[16,32,1024]{2,1,0:T(8,128)(2,1)}), bf16[16,32,1024]{2,1,0:T(8,128)(2,1)S(1)}, u32[]{:S(2)}, u32[]{:S(2)}) async-start(bf16[16,32,1024]{2,1,0:T(8,128)(2,1)} %bitcast.7), calls=%async_computation.2 | async-start | bytes 2097152 | tf_op jit(solution)/shard_map/all_to_all | solution.py:37
  51.6 0.0 reduce-scatter.2.cloned.1.call-start
  51.6 14.1 %all-gather.2.cloned.1.call-done = bf16[1,1024,1408]{2,1,0:T(8,128)(2,1)} async-done(((bf16[1,512,1408]{2,1,0:T(8,128)(2,1)}), bf16[1,1024,1408]{2,1,0:T(8,128)(2,1)}) %all-gather.2.cloned.1.call-update) | async-done | bytes 2883600 | tf_op jit(solution)/shard_map/all_gather | solution.py:41
  65.7 5.5 %fusion.2 = f32[512,1408]{1,0:T(8,128)} fusion(bf16[512,1024]{1,0:T(8,128)(2,1)} %bitcast.2, bf16[1,1024,1408]{2,1,0:T(8,128)(2,1)} %all-gather.2.cloned.1.call-done), kind=kOutput, calls=%fused_computation.7 | convolution fusion | flops 1476395008 | bytes 6815744 | tf_op jit(solution)/shard_map/dot_general | solution.py:42
  71.2 5.3 %all-to-all-done.2 = bf16[16,32,1024]{2,1,0:T(8,128)(2,1)S(1)} async-done(((bf16[16,32,1024]{2,1,0:T(8,128)(2,1)}), bf16[16,32,1024]{2,1,0:T(8,128)(2,1)S(1)}, u32[]{:S(2)}, u32[]{:S(2)}) %all-to-all-start.2) | async-done | bytes 1048608 | tf_op jit(solution)/shard_map/all_to_all | solution.py:37
  76.5 0.0 copy-done
  76.5 3.3 %multiply_convert_fusion.1 = (bf16[512,704]{1,0:T(8,128)(2,1)S(1)}, bf16[512,704]{1,0:T(8,128)(2,1)S(1)}) fusion(f32[512,1408]{1,0:T(8,128)} %fusion.2, bf16[512,1024]{1,0:T(8,128)(2,1)S(1)} %bitcast.53, bf16[1,704,1024]{2,1,0:T(8,128)(2,1)S(1)} %copy-done), kind=kOutput, calls=%fused_computation.11 | convolution fusion | flops 742883328 | bytes 6815744 | tf_op jit(solution)/shard_map/dot_general | solution.py:52
  79.8 0.0 copy-start.4
  79.8 0.9 copy-done.4
  80.7 4.7 %convolution_convert_fusion = bf16[1024,1408]{1,0:T(8,128)(2,1)} fusion(bf16[512,1024]{1,0:T(8,128)(2,1)} %bitcast.2, bf16[512,704]{1,0:T(8,128)(2,1)S(1)} %get-tuple-element.5, bf16[512,704]{1,0:T(8,128)(2,1)S(1)} %get-tuple-element.4), kind=kOutput, calls=%fused_computation.4 | convolution fusion | flops 1480720384 | bytes 5373952 | tf_op jit(solution)/shard_map/dot_general | solution.py:61
  85.3 0.0 reduce-scatter.2.cloned.1.call-update
  85.4 4.0 %convolution_convert_fusion.1 = bf16[512,1024]{1,0:T(8,128)(2,1)} fusion(bf16[1,704,1024]{2,1,0:T(8,128)(2,1)S(1)} %copy-done, f32[512,1408]{1,0:T(8,128)} %fusion.2), kind=kOutput, calls=%fused_computation.17 | convolution fusion | flops 740884480 | bytes 5636096 | tf_op jit(solution)/shard_map/dot_general | solution.py:48
  89.3 4.9 %all-to-all-start.1 = ((bf16[16,32,1024]{2,1,0:T(8,128)(2,1)}), bf16[16,32,1024]{2,1,0:T(8,128)(2,1)S(1)}, u32[]{:S(2)}, u32[]{:S(2)}) async-start(bf16[16,32,1024]{2,1,0:T(8,128)(2,1)} %bitcast.5), calls=%async_computation.1 | async-start | bytes 2097152 | tf_op jit(solution)/shard_map/all_to_all | solution.py:65
  94.3 4.9 %fusion.5 = bf16[512,1024]{1,0:T(8,128)(2,1)} fusion(bf16[1,1024,1408]{2,1,0:T(8,128)(2,1)} %all-gather.2.cloned.1.call-done, bf16[512,704]{1,0:T(8,128)(2,1)} %copy-done.4, bf16[512,704]{1,0:T(8,128)(2,1)S(1)} %get-tuple-element.4), kind=kOutput, calls=%fused_computation.16 | convolution fusion | flops 1479802880 | bytes 5373952 | tf_op jit(solution)/shard_map/dot_general | solution.py:58
  99.2 20.4 %all-to-all-done.1 = bf16[16,32,1024]{2,1,0:T(8,128)(2,1)S(1)} async-done(((bf16[16,32,1024]{2,1,0:T(8,128)(2,1)}), bf16[16,32,1024]{2,1,0:T(8,128)(2,1)S(1)}, u32[]{:S(2)}, u32[]{:S(2)}) %all-to-all-start.1) | async-done | bytes 1048608 | tf_op jit(solution)/shard_map/all_to_all | solution.py:65
  119.6 4.5 %all-to-all-start.3 = ((bf16[16,32,1024]{2,1,0:T(8,128)(2,1)}), bf16[16,32,1024]{2,1,0:T(8,128)(2,1)S(1)}, u32[]{:S(2)}, u32[]{:S(2)}) async-start(bf16[16,32,1024]{2,1,0:T(8,128)(2,1)} %bitcast.54), calls=%async_computation.3 | async-start | bytes 2097152 | tf_op jit(solution)/shard_map/all_to_all | solution.py:72
  124.1 2.7 %gather_fusion = bf16[384,1024]{1,0:T(8,128)(2,1)} fusion(bf16[512,1024]{1,0:T(8,128)(2,1)S(1)} %bitcast.51, s32[1024]{0:T(1024)S(1)} %pad_clamp_fusion), kind=kCustom, calls=%fused_computation | custom fusion | bytes 1574400 | tf_op jit(solution)/shard_map/gather | solution.py:80
  126.8 22.2 %all-to-all-done.3 = bf16[16,32,1024]{2,1,0:T(8,128)(2,1)S(1)} async-done(((bf16[16,32,1024]{2,1,0:T(8,128)(2,1)}), bf16[16,32,1024]{2,1,0:T(8,128)(2,1)S(1)}, u32[]{:S(2)}, u32[]{:S(2)}) %all-to-all-start.3) | async-done | bytes 1048608 | tf_op jit(solution)/shard_map/all_to_all | solution.py:72
  149.0 2.7 %gather_fusion.1 = bf16[384,1024]{1,0:T(8,128)(2,1)} fusion(bf16[512,1024]{1,0:T(8,128)(2,1)S(1)} %bitcast.52, s32[1024]{0:T(1024)S(1)} %pad_clamp_fusion), kind=kCustom, calls=%fused_computation.1 | custom fusion | bytes 1574400 | tf_op jit(solution)/shard_map/gather | solution.py:83
  151.6 0.0 copy-start.2
  151.6 1.4 reshape.100
  153.0 0.0 copy-done.2
  153.0 0.7 fusion.16
  153.8 0.7 copy.23
  154.4 1.3 reshape.105
  155.8 1.4 reduce_sum.35
  157.1 2.2 %multiply_reduce_fusion = bf16[64,1024]{1,0:T(8,128)(2,1)} fusion(bf16[64,6,1024]{2,1,0:T(8,128)(2,1)S(1)} %reshape.100, f32[64,6]{1,0:T(8,128)} %copy-done.1), kind=kLoop, calls=%fused_computation.9 | loop fusion | flops 1114112 | bytes 919040 | tf_op jit(solution)/shard_map/reduce_sum | solution.py:86
  159.3 0.0 reduce-scatter.2.cloned.1.call-done
  (4 shorter events, 0.1 us)
Async XLA Ops:
  7.2 69.3 %copy-start = (bf16[1,704,1024]{2,1,0:T(8,128)(2,1)S(1)}, bf16[1,704,1024]{2,1,0:T(8,128)(2,1)}, u32[]{:S(2)}) copy-start(bf16[1,704,1024]{2,1,0:T(8,128)(2,1)} %param.11) | copy-start | bytes 4325380
  15.0 7.4 %copy-start.3 = (f32[64,6]{0,1:T(8,128)S(1)}, f32[64,6]{0,1:T(8,128)}, u32[]{:S(2)}) copy-start(f32[64,6]{0,1:T(8,128)} %param.9) | copy-start | bytes 4612
  15.0 32.0 %all-to-all-start = ((bf16[16,32,1024]{2,1,0:T(8,128)(2,1)}), bf16[16,32,1024]{2,1,0:T(8,128)(2,1)}, u32[]{:S(2)}, u32[]{:S(2)}) async-start(bf16[16,32,1024]{2,1,0:T(8,128)(2,1)} %bitcast.1), calls=%async_computation | async-start | bytes 2097152 | tf_op jit(solution)/shard_map/all_to_all | solution.py:36
  21.7 44.0 %all-gather.2.cloned.1.call-start = ((), (), s32[]{:S(2)}) async-start(), calls=%async_computation.5 | async-start | bytes 4325376 | tf_op jit(solution)/shard_map/all_gather | solution.py:41
  22.5 0.6 copy-start.1
  46.9 29.5 %all-to-all-start.2 = ((bf16[16,32,1024]{2,1,0:T(8,128)(2,1)}), bf16[16,32,1024]{2,1,0:T(8,128)(2,1)S(1)}, u32[]{:S(2)}, u32[]{:S(2)}) async-start(bf16[16,32,1024]{2,1,0:T(8,128)(2,1)} %bitcast.7), calls=%async_computation.2 | async-start | bytes 2097152 | tf_op jit(solution)/shard_map/all_to_all | solution.py:37
  51.6 107.8 %reduce-scatter.2.cloned.1.call-start = ((), (), s32[]{:S(2)}) async-start(), calls=%async_computation.6 | async-start | bytes 4325376 | tf_op jit(solution)/shard_map/reduce_scatter | solution.py:91
  79.8 0.9 copy-start.4
  89.3 30.2 %all-to-all-start.1 = ((bf16[16,32,1024]{2,1,0:T(8,128)(2,1)}), bf16[16,32,1024]{2,1,0:T(8,128)(2,1)S(1)}, u32[]{:S(2)}, u32[]{:S(2)}) async-start(bf16[16,32,1024]{2,1,0:T(8,128)(2,1)} %bitcast.5), calls=%async_computation.1 | async-start | bytes 2097152 | tf_op jit(solution)/shard_map/all_to_all | solution.py:65
  119.6 29.4 %all-to-all-start.3 = ((bf16[16,32,1024]{2,1,0:T(8,128)(2,1)}), bf16[16,32,1024]{2,1,0:T(8,128)(2,1)S(1)}, u32[]{:S(2)}, u32[]{:S(2)}) async-start(bf16[16,32,1024]{2,1,0:T(8,128)(2,1)} %bitcast.54), calls=%async_computation.3 | async-start | bytes 2097152 | tf_op jit(solution)/shard_map/all_to_all | solution.py:72
  151.6 1.4 copy-start.2
Sparse Core Ops, SparseCore 0:
  24.0 41.6 all-gather.1
  85.5 39.0 reduce-scatter.1
where the time goes:
time: 167 us; the launch traced here: 166 us
  waiting for transfers between devices  79.7 us (48%)
  matrix products  23 us (14%)
  starting transfers between devices  20.9 us (13%)
  local copies, waits for them, and re-layouts  18.9 us (11%)
  between operations  14.2 us (9%)
  other arithmetic  9.39 us (6%)
    all_to_all x1, waiting for transfers between devices, local(): lax.all_to_all(input_cot.reshape(experts, capacity, model_width), 'expert...  22.2 us
    all_to_all x1, waiting for transfers between devices, local(): lax.all_to_all(output_rows.reshape(experts, capacity, model_width), 'expe...  20.4 us
    all_to_all x1, waiting for transfers between devices, local(): lax.all_to_all(token_send, 'expert', split_axis=0, concat_axis=0, tiled=T...  17.2 us
    all_gather x1, waiting for transfers between devices, local(): weight_fwd = lax.all_gather(w_gate_up, 'dp', axis=1, tiled=True)[0]  14.1 us
    all_to_all x1, starting transfers between devices, local(): lax.all_to_all(token_send, 'expert', split_axis=0, concat_axis=0, tiled=T...  6.69 us
    dot_general x1, matrix products, local(): jnp.dot(input_rows, weight_fwd, preferred_element_type=jnp.float32)  5.5 us
    all_to_all x1, waiting for transfers between devices, local(): lax.all_to_all(cot_send, 'expert', split_axis=0, concat_axis=0, tiled=True)  5.26 us
    all_to_all x1, starting transfers between devices, local(): lax.all_to_all(output_rows.reshape(experts, capacity, model_width), 'expe...  4.95 us
  transfers between devices with their start and end apart: 6, of which 5 were waited for; matrix products, arithmetic and copies ran while one was open for 21% of the time, Pallas kernels for 0%

commit v1 on v0

--- a/solution.py
+++ b/solution.py
@@ -2,6 +2,29 @@
 import jax.numpy as jnp
 from jax import lax
 from jax.sharding import PartitionSpec as P
+
+
+def split_up(array, dim, length):
+    shape = array.shape
+    blocks = array.reshape(*shape[:dim], length, shape[dim] // length, *shape[dim + 1 :])
+    return jnp.moveaxis(blocks, dim, 0)
+
+
+def in_order(pieces, dim):
+    shape = list(pieces.shape[1:])
+    shape[dim] *= pieces.shape[0]
+    return jnp.moveaxis(pieces, 0, dim).reshape(shape)
+
+
+def sent_to_each(array, axis, split_dim, concat_dim):
+    size, here = (lax.axis_size(axis), lax.axis_index(axis))
+    tiles = split_up(array, split_dim, size)
+    finished = [tiles[here]]
+    for turn in range(1, size):
+        sent = tiles[(here + turn) % size]
+        finished.append(lax.ppermute(sent, axis, [(i, (i + turn) % size) for i in range(size)]))
+    tiles = jnp.stack(finished)[(here - jnp.arange(size)) % size]
+    return in_order(tiles, concat_dim)
 
 
 def local(tokens, cotangent, expert_ids, gate_probs, w_gate_up, w_down):
@@ -33,7 +56,7 @@
     token_send = token_send.reshape(experts, capacity, model_width)
     cot_send = cot_send.reshape(experts, capacity, model_width)
     token_recv, cot_early = (
-        lax.all_to_all(token_send, "expert", split_axis=0, concat_axis=0, tiled=True),
+        sent_to_each(token_send, "expert", 0, 0),
         lax.all_to_all(cot_send, "expert", split_axis=0, concat_axis=0, tiled=True),
     )
     input_rows = token_recv.reshape(experts * capacity, model_width)

time: 167 us -> 208 us (1.25)
  starting transfers between devices: 20.9 us -> 48.4 us
  waiting for transfers between devices: 79.7 us -> 90.9 us
  local copies, waits for them, and re-layouts: 18.9 us -> 22.9 us
    ppermute x0 -> x15, waiting for transfers between devices: none -> 47.6 us  [sent_to_each(): lax.ppermute(sent, axis, [(i, (i + turn) % size) for i in range(size)])]
    ppermute x0 -> x15, starting transfers between devices: none -> 32.5 us  [sent_to_each(): lax.ppermute(sent, axis, [(i, (i + turn) % size) for i in range(size)])]
    all_to_all x1 -> x0, waiting for transfers between devices: 17.2 us -> none  [local(): lax.all_to_all(token_send, 'expert', split_axis=0, concat_axis=0, tiled=T...]
    all_gather x1, waiting for transfers between devices: 14.1 us -> 0.02 us  [local(): weight_fwd = lax.all_gather(w_gate_up, 'dp', axis=1, tiled=True)[0]]
    all_to_all x1 -> x0, starting transfers between devices: 6.69 us -> none  [local(): lax.all_to_all(token_send, 'expert', split_axis=0, concat_axis=0, tiled=T...]
    all_to_all x1, waiting for transfers between devices: 5.26 us -> 0.01 us  [local(): lax.all_to_all(cot_send, 'expert', split_axis=0, concat_axis=0, tiled=True)]
    unnamed x12 -> x56, local copies, waits for them, and re-layouts: 2.38 us -> 5.43 us
  transfers between devices with their start and end apart: 6 -> 20, of which waited for: 5 -> 12; matrix products, arithmetic and copies ran while one was open for 21% -> 21% of each run, Pallas kernels for 0% -> 0%
where the time goes in v1:
time: 208 us; the launch traced here: 207 us
  waiting for transfers between devices  90.9 us (44%)
  starting transfers between devices  48.4 us (23%)
  local copies, waits for them, and re-layouts  22.9 us (11%)
  matrix products  21.9 us (11%)
  between operations  14.6 us (7%)
  other arithmetic  8.67 us (4%)
    ppermute x15, waiting for transfers between devices, sent_to_each(): lax.ppermute(sent, axis, [(i, (i + turn) % size) for i in range(size)])  47.6 us
    ppermute x15, starting transfers between devices, sent_to_each(): lax.ppermute(sent, axis, [(i, (i + turn) % size) for i in range(size)])  32.5 us
    all_to_all x1, waiting for transfers between devices, local(): lax.all_to_all(input_cot.reshape(experts, capacity, model_width), 'expert...  22.2 us
    all_to_all x1, waiting for transfers between devices, local(): lax.all_to_all(output_rows.reshape(experts, capacity, model_width), 'expe...  20.4 us
    all_to_all x1, starting transfers between devices, local(): lax.all_to_all(output_rows.reshape(experts, capacity, model_width), 'expe...  6.47 us
    unnamed x56, local copies, waits for them, and re-layouts  5.43 us
    dot_general x1, matrix products, local(): jnp.dot(input_rows, weight_fwd, preferred_element_type=jnp.float32)  5.24 us
    dot_general x1, matrix products, local(): lax.dot_general(pair_cot, weight_fwd, (((1,), (1,)), ((), ())), preferred...  4.87 us
  transfers between devices with their start and end apart: 20, of which 12 were waited for; matrix products, arithmetic and copies ran while one was open for 21% of the time, Pallas kernels for 0%

profile of v1, /device:TPU:15, one launch (start us, length us, event | category | flops | bytes accessed | tf_op | source)
XLA Modules:
  0.0 207.4 jit_solution(13331869037245060146)
XLA Ops:
  7.2 0.7 all-gather.2.cloned.1.call-update
  8.2 0.1 eq.47
  8.4 0.1 eq.43
  8.6 0.1 mul.69
  8.8 0.9 reduce-window.6
  9.7 0.2 slice_reduce_fusion
  9.9 0.2 broadcast_in_dim.4
  10.1 0.3 reshape.177
  10.6 2.4 %scatter_custom_fusion = bf16[512,1024]{1,0:T(8,128)(2,1)S(1)} fusion(s32[384]{0:T(512)S(1)} %fusion.23, bf16[384,1024]{1,0:T(8,128)(2,1)S(1)} %reshape.177, bf16[]{:T(256)} %constant.106.clone.1), kind=kCustom, calls=%fused_computation.26 | custom fusion | bytes 1048578 | tf_op jit(solution)/shard_map/scatter | solution.py:51
  12.9 1.0 dynamic-slice_bitcast_fusion
  14.0 0.7 collective-permute-start.14
  14.6 0.3 collective-permute-start.13
  14.9 1.3 collective-permute-start.12
  16.2 3.3 %collective-permute-start.11 = (bf16[1,32,1024]{2,1,0:T(8,128)(2,1)}, bf16[1,32,1024]{2,1,0:T(8,128)(2,1)}, u32[]{:S(2)}, u32[]{:S(2)}) collective-permute-start(bf16[1,32,1024]{2,1,0:T(8,128)(2,1)} %get-tuple-element.9), channel_id=1, source_target_pairs={{0,12},{1,13},{2,14},{3,15},{4,0},{5,1},{6,2},{7,3},{8,4},{9,5},{1... | collective-permute-start | bytes 196616 | tf_op jit(solution)/shard_map/ppermute | solution.py:25
  19.5 1.5 collective-permute-start
  21.1 0.6 copy-done.2
  21.9 1.2 mul.76
  23.1 1.4 mul.77
  24.5 4.1 %scatter_custom_fusion.1 = bf16[512,1024]{1,0:T(8,128)(2,1)} fusion(s32[384]{0:T(512)S(1)} %fusion.23, f32[384,1024]{1,0:T(8,128)} %mul.77, f32[384]{0:T(512)S(1)} %mul.74, bf16[]{:T(256)} %constant.106.clone.1), kind=kCustom, calls=%fused_computation.23 | custom fusion | flops 786432 | bytes 2623490 | tf_op jit(solution)/shard_map/scatter | solution.py:54
  28.6 4.8 %all-to-all-start.1 = ((bf16[16,32,1024]{2,1,0:T(8,128)(2,1)}), bf16[16,32,1024]{2,1,0:T(8,128)(2,1)}, u32[]{:S(2)}, u32[]{:S(2)}) async-start(bf16[16,32,1024]{2,1,0:T(8,128)(2,1)} %bitcast.39), calls=%async_computation.1 | async-start | bytes 2097152 | tf_op jit(solution)/shard_map/all_to_all | solution.py:60
  33.5 1.2 collective-permute-start.1
  34.7 0.8 bitcast_dynamic-update-slice_fusion.14
  35.6 22.0 %collective-permute-done.1 = bf16[1,32,1024]{2,1,0:T(8,128)(2,1)S(1)} collective-permute-done((bf16[1,32,1024]{2,1,0:T(8,128)(2,1)S(1)}, bf16[1,32,1024]{2,1,0:T(8,128)(2,1)S(1)}, u32[]{:S(2)}, u32[]{:S(2)}) %collective-permute-start.1) | collective-permute-done | bytes 65568 | tf_op jit(solution)/shard_map/ppermute | solution.py:25
  57.6 4.0 %collective-permute-done.2 = bf16[1,32,1024]{2,1,0:T(8,128)(2,1)S(1)} collective-permute-done((bf16[1,32,1024]{2,1,0:T(8,128)(2,1)S(1)}, bf16[1,32,1024]{2,1,0:T(8,128)(2,1)S(1)}, u32[]{:S(2)}, u32[]{:S(2)}) %collective-permute-start.2) | collective-permute-done | bytes 65568 | tf_op jit(solution)/shard_map/ppermute | solution.py:25
  61.5 2.1 %collective-permute-start.3 = (bf16[1,32,1024]{2,1,0:T(8,128)(2,1)S(1)}, bf16[1,32,1024]{2,1,0:T(8,128)(2,1)S(1)}, u32[]{:S(2)}, u32[]{:S(2)}) collective-permute-start(bf16[1,32,1024]{2,1,0:T(8,128)(2,1)S(1)} %copy-done.12), channel_id=1, source_target_pairs={{0,4},{1,5},{2,6},{3,7},{4,8},{5,9},{6,10},{7,11},{8,12},{9,13},{1... | collective-permute-start | bytes 196616 | tf_op jit(solution)/shard_map/ppermute | solution.py:25
  63.6 1.4 collective-permute-done.3
  65.1 4.3 %collective-permute-start.4 = (bf16[1,32,1024]{2,1,0:T(8,128)(2,1)S(1)}, bf16[1,32,1024]{2,1,0:T(8,128)(2,1)S(1)}, u32[]{:S(2)}, u32[]{:S(2)}) collective-permute-start(bf16[1,32,1024]{2,1,0:T(8,128)(2,1)S(1)} %copy-done.11), channel_id=1, source_target_pairs={{0,5},{1,6},{2,7},{3,8},{4,9},{5,10},{6,11},{7,12},{8,13},{9,14},{... | collective-permute-start | bytes 196616 | tf_op jit(solution)/shard_map/ppermute | solution.py:25
  69.4 1.3 collective-permute-done.4
  70.7 2.1 %collective-permute-start.5 = (bf16[1,32,1024]{2,1,0:T(8,128)(2,1)S(1)}, bf16[1,32,1024]{2,1,0:T(8,128)(2,1)S(1)}, u32[]{:S(2)}, u32[]{:S(2)}) collective-permute-start(bf16[1,32,1024]{2,1,0:T(8,128)(2,1)S(1)} %copy-done.10), channel_id=1, source_target_pairs={{0,6},{1,7},{2,8},{3,9},{4,10},{5,11},{6,12},{7,13},{8,14},{9,15},... | collective-permute-start | bytes 196616 | tf_op jit(solution)/shard_map/ppermute | solution.py:25
  72.8 3.5 %collective-permute-done.5 = bf16[1,32,1024]{2,1,0:T(8,128)(2,1)S(1)} collective-permute-done((bf16[1,32,1024]{2,1,0:T(8,128)(2,1)S(1)}, bf16[1,32,1024]{2,1,0:T(8,128)(2,1)S(1)}, u32[]{:S(2)}, u32[]{:S(2)}) %collective-permute-start.5) | collective-permute-done | bytes 65568 | tf_op jit(solution)/shard_map/ppermute | solution.py:25
  76.3 2.5 %collective-permute-start.6 = (bf16[1,32,1024]{2,1,0:T(8,128)(2,1)S(1)}, bf16[1,32,1024]{2,1,0:T(8,128)(2,1)S(1)}, u32[]{:S(2)}, u32[]{:S(2)}) collective-permute-start(bf16[1,32,1024]{2,1,0:T(8,128)(2,1)S(1)} %copy-done.9), channel_id=1, source_target_pairs={{0,7},{1,8},{2,9},{3,10},{4,11},{5,12},{6,13},{7,14},{8,15},{9,0},... | collective-permute-start | bytes 196616 | tf_op jit(solution)/shard_map/ppermute | solution.py:25
  78.8 4.9 %collective-permute-done.6 = bf16[1,32,1024]{2,1,0:T(8,128)(2,1)S(1)} collective-permute-done((bf16[1,32,1024]{2,1,0:T(8,128)(2,1)S(1)}, bf16[1,32,1024]{2,1,0:T(8,128)(2,1)S(1)}, u32[]{:S(2)}, u32[]{:S(2)}) %collective-permute-start.6) | collective-permute-done | bytes 65568 | tf_op jit(solution)/shard_map/ppermute | solution.py:25
  83.8 0.6 collective-permute-start.7
  84.4 3.9 %collective-permute-done.7 = bf16[1,32,1024]{2,1,0:T(8,128)(2,1)S(1)} collective-permute-done((bf16[1,32,1024]{2,1,0:T(8,128)(2,1)S(1)}, bf16[1,32,1024]{2,1,0:T(8,128)(2,1)S(1)}, u32[]{:S(2)}, u32[]{:S(2)}) %collective-permute-start.7) | collective-permute-done | bytes 65568 | tf_op jit(solution)/shard_map/ppermute | solution.py:25
  88.3 3.8 %collective-permute-start.8 = (bf16[1,32,1024]{2,1,0:T(8,128)(2,1)S(1)}, bf16[1,32,1024]{2,1,0:T(8,128)(2,1)S(1)}, u32[]{:S(2)}, u32[]{:S(2)}) collective-permute-start(bf16[1,32,1024]{2,1,0:T(8,128)(2,1)S(1)} %copy-done.7), channel_id=1, source_target_pairs={{0,9},{1,10},{2,11},{3,12},{4,13},{5,14},{6,15},{7,0},{8,1},{9,2},... | collective-permute-start | bytes 196616 | tf_op jit(solution)/shard_map/ppermute | solution.py:25
  92.1 1.3 collective-permute-done.8
  93.4 3.7 %collective-permute-start.9 = (bf16[1,32,1024]{2,1,0:T(8,128)(2,1)S(1)}, bf16[1,32,1024]{2,1,0:T(8,128)(2,1)S(1)}, u32[]{:S(2)}, u32[]{:S(2)}) collective-permute-start(bf16[1,32,1024]{2,1,0:T(8,128)(2,1)S(1)} %copy-done.6), channel_id=1, source_target_pairs={{0,10},{1,11},{2,12},{3,13},{4,14},{5,15},{6,0},{7,1},{8,2},{9,3},... | collective-permute-start | bytes 196616 | tf_op jit(solution)/shard_map/ppermute | solution.py:25
  97.1 1.3 collective-permute-done.9
  98.4 5.1 %collective-permute-start.10 = (bf16[1,32,1024]{2,1,0:T(8,128)(2,1)S(1)}, bf16[1,32,1024]{2,1,0:T(8,128)(2,1)S(1)}, u32[]{:S(2)}, u32[]{:S(2)}) collective-permute-start(bf16[1,32,1024]{2,1,0:T(8,128)(2,1)S(1)} %copy-done.5), channel_id=1, source_target_pairs={{0,11},{1,12},{2,13},{3,14},{4,15},{5,0},{6,1},{7,2},{8,3},{9,4},{... | collective-permute-start | bytes 196616 | tf_op jit(solution)/shard_map/ppermute | solution.py:25
  103.6 3.9 %collective-permute-done.10 = bf16[1,32,1024]{2,1,0:T(8,128)(2,1)S(1)} collective-permute-done((bf16[1,32,1024]{2,1,0:T(8,128)(2,1)S(1)}, bf16[1,32,1024]{2,1,0:T(8,128)(2,1)S(1)}, u32[]{:S(2)}, u32[]{:S(2)}) %collective-permute-start.10) | collective-permute-done | bytes 65568 | tf_op jit(solution)/shard_map/ppermute | solution.py:25
  107.5 0.8 bitcast_dynamic-update-slice_fusion.3
  108.4 0.8 bitcast_dynamic-update-slice_fusion.2
  109.2 0.8 bitcast_dynamic-update-slice_fusion.1
  110.0 0.8 bitcast_dynamic-update-slice_fusion
  110.9 0.6 gather_fusion
  111.5 5.2 %fusion.2 = f32[512,1408]{1,0:T(8,128)} fusion(bf16[512,1024]{1,0:T(8,128)(2,1)S(1)} %bitcast.118, bf16[1,1024,1408]{2,1,0:T(8,128)(2,1)} %all-gather.2.cloned.1.call-done), kind=kOutput, calls=%fused_computation.8 | convolution fusion | flops 1476395008 | bytes 6815744 | tf_op jit(solution)/shard_map/dot_general | solution.py:65
  116.8 3.6 %multiply_convert_fusion.1 = (bf16[512,704]{1,0:T(8,128)(2,1)S(1)}, bf16[512,704]{1,0:T(8,128)(2,1)S(1)}) fusion(f32[512,1408]{1,0:T(8,128)} %fusion.2, bf16[512,1024]{1,0:T(8,128)(2,1)} %bitcast.40, bf16[1,704,1024]{2,1,0:T(8,128)(2,1)S(1)} %copy-done), kind=kOutput, calls=%fused_computation.12 | convolution fusion | flops 742883328 | bytes 6815744 | tf_op jit(solution)/shard_map/dot_general | solution.py:75
  120.4 0.9 copy-done.17
  121.3 0.3 copy-done.19
  121.6 3.5 %convolution_convert_fusion = bf16[1024,1408]{1,0:T(8,128)(2,1)} fusion(bf16[512,1024]{1,0:T(8,128)(2,1)S(1)} %bitcast.119, bf16[512,704]{1,0:T(8,128)(2,1)S(1)} %get-tuple-element.5, bf16[512,704]{1,0:T(8,128)(2,1)S(1)} %get-tuple-element.4), kind=kOutput, calls=%fused_computation.5 | convolution fusion | flops 1480720384 | bytes 5373952 | tf_op jit(solution)/shard_map/dot_general | solution.py:84
  125.1 3.9 %convolution_convert_fusion.1 = bf16[512,1024]{1,0:T(8,128)(2,1)} fusion(bf16[1,704,1024]{2,1,0:T(8,128)(2,1)S(1)} %copy-done, f32[512,1408]{1,0:T(8,128)} %fusion.2), kind=kOutput, calls=%fused_computation.18 | convolution fusion | flops 740884480 | bytes 5636096 | tf_op jit(solution)/shard_map/dot_general | solution.py:71
  129.0 6.5 %all-to-all-start = ((bf16[16,32,1024]{2,1,0:T(8,128)(2,1)}), bf16[16,32,1024]{2,1,0:T(8,128)(2,1)S(1)}, u32[]{:S(2)}, u32[]{:S(2)}) async-start(bf16[16,32,1024]{2,1,0:T(8,128)(2,1)} %bitcast.37), calls=%async_computation | async-start | bytes 2097152 | tf_op jit(solution)/shard_map/all_to_all | solution.py:88
  135.5 4.9 %fusion.5 = bf16[512,1024]{1,0:T(8,128)(2,1)} fusion(bf16[1,1024,1408]{2,1,0:T(8,128)(2,1)} %all-gather.2.cloned.1.call-done, bf16[512,704]{1,0:T(8,128)(2,1)} %copy-done.19, bf16[512,704]{1,0:T(8,128)(2,1)S(1)} %copy-done.18), kind=kOutput, calls=%fused_computation.17 | convolution fusion | flops 1479802880 | bytes 5373952 | tf_op jit(solution)/shard_map/dot_general | solution.py:81
  140.3 20.4 %all-to-all-done = bf16[16,32,1024]{2,1,0:T(8,128)(2,1)S(1)} async-done(((bf16[16,32,1024]{2,1,0:T(8,128)(2,1)}), bf16[16,32,1024]{2,1,0:T(8,128)(2,1)S(1)}, u32[]{:S(2)}, u32[]{:S(2)}) %all-to-all-start) | async-done | bytes 1048608 | tf_op jit(solution)/shard_map/all_to_all | solution.py:88
  160.7 4.5 %all-to-all-start.2 = ((bf16[16,32,1024]{2,1,0:T(8,128)(2,1)}), bf16[16,32,1024]{2,1,0:T(8,128)(2,1)S(1)}, u32[]{:S(2)}, u32[]{:S(2)}) async-start(bf16[16,32,1024]{2,1,0:T(8,128)(2,1)} %bitcast.120), calls=%async_computation.2 | async-start | bytes 2097152 | tf_op jit(solution)/shard_map/all_to_all | solution.py:95
  165.3 2.7 %gather_fusion.1 = bf16[384,1024]{1,0:T(8,128)(2,1)} fusion(bf16[512,1024]{1,0:T(8,128)(2,1)S(1)} %bitcast.114, s32[1024]{0:T(1024)S(1)} %pad_clamp_fusion), kind=kCustom, calls=%fused_computation.1 | custom fusion | bytes 1574400 | tf_op jit(solution)/shard_map/gather | solution.py:103
  168.0 22.2 %all-to-all-done.2 = bf16[16,32,1024]{2,1,0:T(8,128)(2,1)S(1)} async-done(((bf16[16,32,1024]{2,1,0:T(8,128)(2,1)}), bf16[16,32,1024]{2,1,0:T(8,128)(2,1)S(1)}, u32[]{:S(2)}, u32[]{:S(2)}) %all-to-all-start.2) | async-done | bytes 1048608 | tf_op jit(solution)/shard_map/all_to_all | solution.py:95
  190.2 2.7 %gather_fusion.2 = bf16[384,1024]{1,0:T(8,128)(2,1)} fusion(bf16[512,1024]{1,0:T(8,128)(2,1)S(1)} %bitcast.115, s32[1024]{0:T(1024)S(1)} %pad_clamp_fusion), kind=kCustom, calls=%fused_computation.2 | custom fusion | bytes 1574400 | tf_op jit(solution)/shard_map/gather | solution.py:106
  192.8 1.4 reshape.141
  194.2 0.7 fusion.16
  194.9 0.7 copy.23
  195.6 1.3 reshape.146
  197.0 1.4 reduce_sum.35
  198.3 2.2 %multiply_reduce_fusion = bf16[64,1024]{1,0:T(8,128)(2,1)} fusion(bf16[64,6,1024]{2,1,0:T(8,128)(2,1)S(1)} %reshape.141, f32[64,6]{1,0:T(8,128)} %copy-done.2), kind=kLoop, calls=%fused_computation.10 | loop fusion | flops 1114112 | bytes 919040 | tf_op jit(solution)/shard_map/reduce_sum | solution.py:109
  (71 shorter events, 0.9 us)
Async XLA Ops:
  7.2 109.6 %copy-start = (bf16[1,704,1024]{2,1,0:T(8,128)(2,1)S(1)}, bf16[1,704,1024]{2,1,0:T(8,128)(2,1)}, u32[]{:S(2)}) copy-start(bf16[1,704,1024]{2,1,0:T(8,128)(2,1)} %param.11) | copy-start | bytes 4325380
  7.2 1.0 copy-start.15
  7.2 2.7 %copy-start.3 = (bf16[64,1024]{1,0:T(8,128)(2,1)S(1)}, bf16[64,1024]{1,0:T(8,128)(2,1)}, u32[]{:S(2)}) copy-start(bf16[64,1024]{1,0:T(8,128)(2,1)} %param.6) | copy-start | bytes 393220
  7.2 104.3 %all-gather.2.cloned.1.call-start = ((), (), s32[]{:S(2)}) async-start(), calls=%async_computation.4 | async-start | bytes 4325376 | tf_op jit(solution)/shard_map/all_gather | solution.py:64
  10.6 10.5 %copy-start.16 = (f32[64,6]{0,1:T(8,128)S(1)}, f32[64,6]{0,1:T(8,128)}, u32[]{:S(2)}) copy-start(f32[64,6]{0,1:T(8,128)} %param.9) | copy-start | bytes 4612
  14.0 96.1 %collective-permute-start.14 = (bf16[1,32,1024]{2,1,0:T(8,128)(2,1)}, bf16[1,32,1024]{2,1,0:T(8,128)(2,1)}, u32[]{:S(2)}, u32[]{:S(2)}) collective-permute-start(bf16[1,32,1024]{2,1,0:T(8,128)(2,1)} %get-tuple-element.6), channel_id=1, source_target_pairs={{0,15},{1,0},{2,1},{3,2},{4,3},{5,4},{6,5},{7,6},{8,7},{9,8},{10,9... | collective-permute-start | bytes 196616 | tf_op jit(solution)/shard_map/ppermute | solution.py:25
  14.6 94.6 %collective-permute-start.13 = (bf16[1,32,1024]{2,1,0:T(8,128)(2,1)}, bf16[1,32,1024]{2,1,0:T(8,128)(2,1)}, u32[]{:S(2)}, u32[]{:S(2)}) collective-permute-start(bf16[1,32,1024]{2,1,0:T(8,128)(2,1)} %get-tuple-element.7), channel_id=1, source_target_pairs={{0,14},{1,15},{2,0},{3,1},{4,2},{5,3},{6,4},{7,5},{8,6},{9,7},{10,... | collective-permute-start | bytes 196616 | tf_op jit(solution)/shard_map/ppermute | solution.py:25
  14.9 93.5 %collective-permute-start.12 = (bf16[1,32,1024]{2,1,0:T(8,128)(2,1)}, bf16[1,32,1024]{2,1,0:T(8,128)(2,1)}, u32[]{:S(2)}, u32[]{:S(2)}) collective-permute-start(bf16[1,32,1024]{2,1,0:T(8,128)(2,1)} %get-tuple-element.8), channel_id=1, source_target_pairs={{0,13},{1,14},{2,15},{3,0},{4,1},{5,2},{6,3},{7,4},{8,5},{9,6},{10... | collective-permute-start | bytes 196616 | tf_op jit(solution)/shard_map/ppermute | solution.py:25
  16.2 91.3 %collective-permute-start.11 = (bf16[1,32,1024]{2,1,0:T(8,128)(2,1)}, bf16[1,32,1024]{2,1,0:T(8,128)(2,1)}, u32[]{:S(2)}, u32[]{:S(2)}) collective-permute-start(bf16[1,32,1024]{2,1,0:T(8,128)(2,1)} %get-tuple-element.9), channel_id=1, source_target_pairs={{0,12},{1,13},{2,14},{3,15},{4,0},{5,1},{6,2},{7,3},{8,4},{9,5},{1... | collective-permute-start | bytes 196616 | tf_op jit(solution)/shard_map/ppermute | solution.py:25
  19.5 14.0 %collective-permute-start = (bf16[1,32,1024]{2,1,0:T(8,128)(2,1)}, bf16[1,32,1024]{2,1,0:T(8,128)(2,1)}, u32[]{:S(2)}, u32[]{:S(2)}) collective-permute-start(bf16[1,32,1024]{2,1,0:T(8,128)(2,1)} %get-tuple-element.20), channel_id=1, source_target_pairs={{0,1},{1,2},{2,3},{3,4},{4,5},{5,6},{6,7},{7,8},{8,9},{9,10},{10,1... | collective-permute-start | bytes 196616 | tf_op jit(solution)/shard_map/ppermute | solution.py:25
  21.1 0.6 copy-start.2
  28.5 5.0 %copy-start.14 = (bf16[1,32,1024]{2,1,0:T(8,128)(2,1)S(1)}, bf16[1,32,1024]{2,1,0:T(8,128)(2,1)}, u32[]{:S(2)}) copy-start(bf16[1,32,1024]{2,1,0:T(8,128)(2,1)} %get-tuple-element.19) | copy-start | bytes 196612
  28.5 6.2 %copy-start.1 = (bf16[16,1,32,1024]{3,2,0,1:T(8,128)(2,1)S(1)}, bf16[16,1,32,1024]{3,2,0,1:T(8,128)(2,1)}, u32[]{:S(2)}) copy-start(bf16[16,1,32,1024]{3,2,0,1:T(8,128)(2,1)} %get-tuple-element.21) | copy-start | bytes 3145732
  28.5 29.0 %copy-start.13 = (bf16[1,32,1024]{2,1,0:T(8,128)(2,1)S(1)}, bf16[1,32,1024]{2,1,0:T(8,128)(2,1)}, u32[]{:S(2)}) copy-start(bf16[1,32,1024]{2,1,0:T(8,128)(2,1)} %get-tuple-element.18) | copy-start | bytes 196612
  28.5 33.0 %copy-start.12 = (bf16[1,32,1024]{2,1,0:T(8,128)(2,1)S(1)}, bf16[1,32,1024]{2,1,0:T(8,128)(2,1)}, u32[]{:S(2)}) copy-start(bf16[1,32,1024]{2,1,0:T(8,128)(2,1)} %get-tuple-element.17) | copy-start | bytes 196612
  28.5 36.5 %copy-start.11 = (bf16[1,32,1024]{2,1,0:T(8,128)(2,1)S(1)}, bf16[1,32,1024]{2,1,0:T(8,128)(2,1)}, u32[]{:S(2)}) copy-start(bf16[1,32,1024]{2,1,0:T(8,128)(2,1)} %get-tuple-element.16) | copy-start | bytes 196612
  28.5 42.2 %copy-start.10 = (bf16[1,32,1024]{2,1,0:T(8,128)(2,1)S(1)}, bf16[1,32,1024]{2,1,0:T(8,128)(2,1)}, u32[]{:S(2)}) copy-start(bf16[1,32,1024]{2,1,0:T(8,128)(2,1)} %get-tuple-element.15) | copy-start | bytes 196612
  28.6 47.8 %copy-start.9 = (bf16[1,32,1024]{2,1,0:T(8,128)(2,1)S(1)}, bf16[1,32,1024]{2,1,0:T(8,128)(2,1)}, u32[]{:S(2)}) copy-start(bf16[1,32,1024]{2,1,0:T(8,128)(2,1)} %get-tuple-element.14) | copy-start | bytes 196612
  28.6 55.2 %copy-start.8 = (bf16[1,32,1024]{2,1,0:T(8,128)(2,1)S(1)}, bf16[1,32,1024]{2,1,0:T(8,128)(2,1)}, u32[]{:S(2)}) copy-start(bf16[1,32,1024]{2,1,0:T(8,128)(2,1)} %get-tuple-element.13) | copy-start | bytes 196612
  28.6 59.7 %copy-start.7 = (bf16[1,32,1024]{2,1,0:T(8,128)(2,1)S(1)}, bf16[1,32,1024]{2,1,0:T(8,128)(2,1)}, u32[]{:S(2)}) copy-start(bf16[1,32,1024]{2,1,0:T(8,128)(2,1)} %get-tuple-element.12) | copy-start | bytes 196612
  28.6 64.8 %copy-start.6 = (bf16[1,32,1024]{2,1,0:T(8,128)(2,1)S(1)}, bf16[1,32,1024]{2,1,0:T(8,128)(2,1)}, u32[]{:S(2)}) copy-start(bf16[1,32,1024]{2,1,0:T(8,128)(2,1)} %get-tuple-element.11) | copy-start | bytes 196612
  28.6 69.8 %copy-start.5 = (bf16[1,32,1024]{2,1,0:T(8,128)(2,1)S(1)}, bf16[1,32,1024]{2,1,0:T(8,128)(2,1)}, u32[]{:S(2)}) copy-start(bf16[1,32,1024]{2,1,0:T(8,128)(2,1)} %get-tuple-element.10) | copy-start | bytes 196612
  28.6 88.2 %all-to-all-start.1 = ((bf16[16,32,1024]{2,1,0:T(8,128)(2,1)}), bf16[16,32,1024]{2,1,0:T(8,128)(2,1)}, u32[]{:S(2)}, u32[]{:S(2)}) async-start(bf16[16,32,1024]{2,1,0:T(8,128)(2,1)} %bitcast.39), calls=%async_computation.1 | async-start | bytes 2097152 | tf_op jit(solution)/shard_map/all_to_all | solution.py:60
  33.4 167.1 %reduce-scatter.2.cloned.1.call-start = ((), (), s32[]{:S(2)}) async-start(), calls=%async_computation.5 | async-start | bytes 4325376 | tf_op jit(solution)/shard_map/reduce_scatter | solution.py:114
  33.5 24.1 %collective-permute-start.1 = (bf16[1,32,1024]{2,1,0:T(8,128)(2,1)S(1)}, bf16[1,32,1024]{2,1,0:T(8,128)(2,1)S(1)}, u32[]{:S(2)}, u32[]{:S(2)}) collective-permute-start(bf16[1,32,1024]{2,1,0:T(8,128)(2,1)S(1)} %copy-done.14), channel_id=1, source_target_pairs={{0,2},{1,3},{2,4},{3,5},{4,6},{5,7},{6,8},{7,9},{8,10},{9,11},{10,... | collective-permute-start | bytes 196616 | tf_op jit(solution)/shard_map/ppermute | solution.py:25
  57.5 4.0 %collective-permute-start.2 = (bf16[1,32,1024]{2,1,0:T(8,128)(2,1)S(1)}, bf16[1,32,1024]{2,1,0:T(8,128)(2,1)S(1)}, u32[]{:S(2)}, u32[]{:S(2)}) collective-permute-start(bf16[1,32,1024]{2,1,0:T(8,128)(2,1)S(1)} %copy-done.13), channel_id=1, source_target_pairs={{0,3},{1,4},{2,5},{3,6},{4,7},{5,8},{6,9},{7,10},{8,11},{9,12},{10... | collective-permute-start | bytes 196616 | tf_op jit(solution)/shard_map/ppermute | solution.py:25
  61.5 3.5 %collective-permute-start.3 = (bf16[1,32,1024]{2,1,0:T(8,128)(2,1)S(1)}, bf16[1,32,1024]{2,1,0:T(8,128)(2,1)S(1)}, u32[]{:S(2)}, u32[]{:S(2)}) collective-permute-start(bf16[1,32,1024]{2,1,0:T(8,128)(2,1)S(1)} %copy-done.12), channel_id=1, source_target_pairs={{0,4},{1,5},{2,6},{3,7},{4,8},{5,9},{6,10},{7,11},{8,12},{9,13},{1... | collective-permute-start | bytes 196616 | tf_op jit(solution)/shard_map/ppermute | solution.py:25
  65.1 5.6 %collective-permute-start.4 = (bf16[1,32,1024]{2,1,0:T(8,128)(2,1)S(1)}, bf16[1,32,1024]{2,1,0:T(8,128)(2,1)S(1)}, u32[]{:S(2)}, u32[]{:S(2)}) collective-permute-start(bf16[1,32,1024]{2,1,0:T(8,128)(2,1)S(1)} %copy-done.11), channel_id=1, source_target_pairs={{0,5},{1,6},{2,7},{3,8},{4,9},{5,10},{6,11},{7,12},{8,13},{9,14},{... | collective-permute-start | bytes 196616 | tf_op jit(solution)/shard_map/ppermute | solution.py:25
  70.7 5.6 %collective-permute-start.5 = (bf16[1,32,1024]{2,1,0:T(8,128)(2,1)S(1)}, bf16[1,32,1024]{2,1,0:T(8,128)(2,1)S(1)}, u32[]{:S(2)}, u32[]{:S(2)}) collective-permute-start(bf16[1,32,1024]{2,1,0:T(8,128)(2,1)S(1)} %copy-done.10), channel_id=1, source_target_pairs={{0,6},{1,7},{2,8},{3,9},{4,10},{5,11},{6,12},{7,13},{8,14},{9,15},... | collective-permute-start | bytes 196616 | tf_op jit(solution)/shard_map/ppermute | solution.py:25
  76.3 7.4 %collective-permute-start.6 = (bf16[1,32,1024]{2,1,0:T(8,128)(2,1)S(1)}, bf16[1,32,1024]{2,1,0:T(8,128)(2,1)S(1)}, u32[]{:S(2)}, u32[]{:S(2)}) collective-permute-start(bf16[1,32,1024]{2,1,0:T(8,128)(2,1)S(1)} %copy-done.9), channel_id=1, source_target_pairs={{0,7},{1,8},{2,9},{3,10},{4,11},{5,12},{6,13},{7,14},{8,15},{9,0},... | collective-permute-start | bytes 196616 | tf_op jit(solution)/shard_map/ppermute | solution.py:25
  83.8 4.5 %collective-permute-start.7 = (bf16[1,32,1024]{2,1,0:T(8,128)(2,1)S(1)}, bf16[1,32,1024]{2,1,0:T(8,128)(2,1)S(1)}, u32[]{:S(2)}, u32[]{:S(2)}) collective-permute-start(bf16[1,32,1024]{2,1,0:T(8,128)(2,1)S(1)} %copy-done.8), channel_id=1, source_target_pairs={{0,8},{1,9},{2,10},{3,11},{4,12},{5,13},{6,14},{7,15},{8,0},{9,1},... | collective-permute-start | bytes 196616 | tf_op jit(solution)/shard_map/ppermute | solution.py:25
  88.3 5.1 %collective-permute-start.8 = (bf16[1,32,1024]{2,1,0:T(8,128)(2,1)S(1)}, bf16[1,32,1024]{2,1,0:T(8,128)(2,1)S(1)}, u32[]{:S(2)}, u32[]{:S(2)}) collective-permute-start(bf16[1,32,1024]{2,1,0:T(8,128)(2,1)S(1)} %copy-done.7), channel_id=1, source_target_pairs={{0,9},{1,10},{2,11},{3,12},{4,13},{5,14},{6,15},{7,0},{8,1},{9,2},... | collective-permute-start | bytes 196616 | tf_op jit(solution)/shard_map/ppermute | solution.py:25
  93.4 5.0 %collective-permute-start.9 = (bf16[1,32,1024]{2,1,0:T(8,128)(2,1)S(1)}, bf16[1,32,1024]{2,1,0:T(8,128)(2,1)S(1)}, u32[]{:S(2)}, u32[]{:S(2)}) collective-permute-start(bf16[1,32,1024]{2,1,0:T(8,128)(2,1)S(1)} %copy-done.6), channel_id=1, source_target_pairs={{0,10},{1,11},{2,12},{3,13},{4,14},{5,15},{6,0},{7,1},{8,2},{9,3},... | collective-permute-start | bytes 196616 | tf_op jit(solution)/shard_map/ppermute | solution.py:25
  98.4 9.1 %collective-permute-start.10 = (bf16[1,32,1024]{2,1,0:T(8,128)(2,1)S(1)}, bf16[1,32,1024]{2,1,0:T(8,128)(2,1)S(1)}, u32[]{:S(2)}, u32[]{:S(2)}) collective-permute-start(bf16[1,32,1024]{2,1,0:T(8,128)(2,1)S(1)} %copy-done.5), channel_id=1, source_target_pairs={{0,11},{1,12},{2,13},{3,14},{4,15},{5,0},{6,1},{7,2},{8,3},{9,4},{... | collective-permute-start | bytes 196616 | tf_op jit(solution)/shard_map/ppermute | solution.py:25
  120.4 0.9 copy-start.17
  120.4 1.1 copy-start.19
  129.0 6.5 %copy-start.18 = (bf16[512,704]{1,0:T(8,128)(2,1)S(1)}, bf16[512,704]{1,0:T(8,128)(2,1)}, u32[]{:S(2)}) copy-start(bf16[512,704]{1,0:T(8,128)(2,1)} %copy-done.17) | copy-start | bytes 2162692
  129.0 31.7 %all-to-all-start = ((bf16[16,32,1024]{2,1,0:T(8,128)(2,1)}), bf16[16,32,1024]{2,1,0:T(8,128)(2,1)S(1)}, u32[]{:S(2)}, u32[]{:S(2)}) async-start(bf16[16,32,1024]{2,1,0:T(8,128)(2,1)} %bitcast.37), calls=%async_computation | async-start | bytes 2097152 | tf_op jit(solution)/shard_map/all_to_all | solution.py:88
  160.7 29.4 %all-to-all-start.2 = ((bf16[16,32,1024]{2,1,0:T(8,128)(2,1)}), bf16[16,32,1024]{2,1,0:T(8,128)(2,1)S(1)}, u32[]{:S(2)}, u32[]{:S(2)}) async-start(bf16[16,32,1024]{2,1,0:T(8,128)(2,1)} %bitcast.120), calls=%async_computation.2 | async-start | bytes 2097152 | tf_op jit(solution)/shard_map/all_to_all | solution.py:95
  192.8 1.4 copy-start.4
Sparse Core Ops, SparseCore 0:
  9.6 42.1 all-gather.1
  125.2 40.4 reduce-scatter.1
